TPU v7x, 512 devices: a whole 4x4x16 slice. The times are simulated.
512 devices in a mesh: space: 32 (over z_lo, x), scal: 16 (over y, z_hi, core).
Axes of the slice: x: 4, y: 4, z: 16 (z_hi: 2, z_lo: 8; z = z_hi * 8 + z_lo), core: 2. Of those that a mesh axis runs over, the one named last changes fastest.
Arguments:
- scalars: float32 [512, 2048, 256], P('scal', 'space'), may hold values from -6 to 6
- schmidt: float32 [512], P('scal'), may hold values from 1 to 1000
- velocity_history: bfloat16 [32, 2, 256, 256], P('scal', None, 'space'), may hold values from -0.796875 to 0.796875
- fine_src: int32 [2048], replicated, may hold values from 0 to 254, as said below
- remap_weight: float32 [2048], replicated, may hold values from 0 to 1
- snap_step: int32 [2], replicated, may hold values from 0 to 31
Outputs:
- transported: float32 [512, 2048, 256], P('scal', 'space')
Inputs may be any that keep to these rules, and one draw needn't show every extreme that they name: fine_src may name any coarse row of any tile, in no particular order.
All inputs are finite; a program needn't handle non-finite values.
Results may differ from a plain program's by a relative error of at most 0.0003.
Values may be sent and summed in bfloat16 or wider, within the bound.
No kernel may reach another device: no remote copies, remote signals or barrier semaphores. Data moves between devices by JAX's collectives and lax.ppermute only.
A program may use at most 64 MiB of HBM per device.

v0:
```python
import jax
import jax.numpy as jnp
from jax import lax
from jax.sharding import PartitionSpec as P

STEPS = 2
diffusion_scale = 0.24


def from_root(value, axis, source):
    kept = jnp.where(lax.axis_index(axis) == source, value, 0).astype(value.dtype)
    return lax.psum(kept, axis)


def padded_2(cells, sides, width):
    for axis, dim in sides:
        count = lax.axis_size(axis)
        ends = count - 1
        head = lax.slice_in_dim(cells, 0, width, axis=dim)
        tail = lax.slice_in_dim(cells, cells.shape[dim] - width, cells.shape[dim], axis=dim)
        cells = jnp.concatenate(
            [
                lax.ppermute(tail, axis, [(i, (i + 1) % count) for i in range(ends)]),
                cells,
                lax.ppermute(head, axis, [((i + 1) % count, i) for i in range(ends)]),
            ],
            axis=dim,
        )
    return cells


def advance(padded, velocity, diffusivity):
    center = padded[:, 1:-1]
    upper_row = padded[:, 2:]
    lower_row = padded[:, :-2]
    east_cell = jnp.roll(center, -1, axis=2)
    west_cell = jnp.roll(center, 1, axis=2)
    laplacian = upper_row + lower_row + east_cell + west_cell - 4.0 * center
    return (
        center
        - velocity[0] * (0.5 * (upper_row - lower_row))
        - velocity[1] * (0.5 * (east_cell - west_cell))
        + diffusivity[:, None, None] * laplacian
    )


def body(scalars, schmidt, velocity_history, fine_src, remap_weight, snap_step):
    tile_rows = scalars.shape[1]
    snap_dev = velocity_history.shape[0]
    coarse_dev = velocity_history.shape[2]
    tile_count = lax.axis_size("space")
    coarse_total = coarse_dev * tile_count
    anchor = lax.axis_index("space") * tile_rows
    diffusivity = diffusion_scale / schmidt
    padded_src = jnp.pad(fine_src, (1, 1))
    padded_weight = jnp.pad(remap_weight, (1, 1))
    field = scalars
    for step_index in range(STEPS):
        padded = padded_2(field, (("space", 1),), 1)
        row_count = tile_rows + 2 * 0
        source_rows = lax.dynamic_slice_in_dim(padded_src, anchor + 1 - 0, row_count)
        weights = lax.dynamic_slice_in_dim(padded_weight, anchor + 1 - 0, row_count)
        coarse_index = lax.broadcasted_iota(jnp.int32, (row_count, coarse_total), 1)
        selection = jnp.where(
            coarse_index == source_rows[:, None], (1.0 - weights)[:, None], 0.0
        ) + jnp.where(coarse_index == source_rows[:, None] + 1, weights[:, None], 0.0)
        snapshot = snap_step[step_index]
        owner_index = snapshot // snap_dev
        own_slot = lax.dynamic_index_in_dim(
            velocity_history, snapshot % snap_dev, 0, keepdims=False
        )
        fine_velocity = jnp.einsum(
            "rn,cnz->crz",
            selection,
            lax.all_gather(own_slot, "space", axis=1, tiled=True).astype(jnp.float32),
            precision=lax.Precision.HIGHEST,
        )
        result_velocity = from_root(fine_velocity, "scal", owner_index)
        field = advance(padded, result_velocity, diffusivity)
    return field


def solution(mesh):
    return jax.shard_map(
        body,
        mesh=mesh,
        in_specs=(
            P("scal", "space", None),
            P("scal"),
            P("scal", None, "space", None),
            P(),
            P(),
            P(),
        ),
        out_specs=P("scal", "space", None),
        check_vma=False,
    )
```

profile of v0, /device:TPU:102, one launch (start us, length us, event | category | flops | bytes accessed | tf_op | source)
XLA Modules:
  0.0 541.2 jit_solution(13713053260277822044)
XLA Ops:
  6.5 0.0 all-reduce.5.cloned.1.call-start
  6.5 1.1 fusion.25
  7.6 5.0 collective-permute-start.1
  12.6 1.9 collective-permute-start
  14.5 1.3 fusion.28
  21.0 0.8 broadcast_add_fusion
  21.7 0.8 broadcast_subtract_fusion
  22.5 0.8 constant_dynamic-slice_fusion
  23.3 71.4 %all-gather.1 = bf16[1,2,256,256]{3,2,1,0:T(8,128)(2,1)S(1)} all-gather(bf16[1,2,8,256]{3,2,1,0:T(8,128)(2,1)S(1)} %get-tuple-element.27), channel_id=3, replica_groups=mesh['space'=32,'scal'=16] {'space'}, dimensions={2}, use_global_device_ids=true | all-gather | bytes 270336 | tf_op jit(solution)/shard_map/all_gather | solution.py:75
  94.7 105.4 %all-gather = bf16[1,2,256,256]{3,2,1,0:T(8,128)(2,1)S(1)} all-gather(bf16[1,2,8,256]{3,2,1,0:T(8,128)(2,1)S(1)} %get-tuple-element.28), channel_id=2, replica_groups=mesh['space'=32,'scal'=16] {'space'}, dimensions={2}, use_global_device_ids=true | all-gather | bytes 270336 | tf_op jit(solution)/shard_map/all_gather | solution.py:75
  200.1 0.9 fusion
  201.1 0.9 fusion.1
  202.0 0.0 all-reduce.5.cloned.1.call-update
  202.0 0.0 copy-start
  202.0 5.1 fusion.26
  207.1 0.0 copy-done
  207.1 0.0 copy-start.2
  207.1 1.4 fusion.27
  208.5 0.0 copy-done.2
  208.5 303.0 %all-reduce.5.cloned.1.call-done = (f32[2,64,256]{2,1,0:T(8,128)}, f32[2,64,256]{2,1,0:T(8,128)}) async-done(((f32[2,64,256]{2,1,0:T(8,128)}, f32[2,64,256]{2,1,0:T(8,128)}), (f32[2,64,256]{2,1,0:T(8,128)}, f32[2,64,256]{2,1,0:T(8,128)})) %all-reduce.5.cloned.1.call-update) | async-done | bytes 262160 | tf_op jit(solution)/shard_map/psum | solution.py:12
  511.4 0.9 fusion.7
  512.3 0.0 collective-permute-done.1
  512.3 0.0 collective-permute-done
  512.4 3.8 multiply_add_fusion.1
  516.2 0.4 fusion.24
  516.6 0.0 copy-start.1
  516.6 0.7 fusion.23
  517.4 4.7 collective-permute-start.3
  522.1 1.9 collective-permute-start.2
  524.0 0.0 copy-done.1
  524.0 0.0 collective-permute-done.3
  524.1 7.2 %collective-permute-done.2 = f32[32,1,256]{2,1,0:T(1,128)S(1)} collective-permute-done((f32[32,1,256]{2,1,0:T(1,128)S(1)}, f32[32,1,256]{2,1,0:T(1,128)S(1)}, u32[]{:S(2)}, u32[]{:S(2)}) %collective-permute-start.2) | collective-permute-done | bytes 32800 | tf_op jit(solution)/shard_map/ppermute | solution.py:25
  531.2 3.1 multiply_add_fusion
  (3 shorter events, 0.1 us)
Async XLA Ops:
  6.5 504.9 %all-reduce.5.cloned.1.call-start = ((), (), s32[]{:S(2)}) async-start(), calls=%async_computation | async-start | bytes 524288 | tf_op jit(solution)/shard_map/psum | solution.py:12
  7.6 504.7 %collective-permute-start.1 = (f32[32,1,256]{2,1,0:T(1,128)S(1)}, f32[32,1,256]{2,1,0:T(1,128)S(1)}, u32[]{:S(2)}, u32[]{:S(2)}) collective-permute-start(f32[32,1,256]{2,1,0:T(1,128)S(1)} %get-tuple-element.17), channel_id=1, source_target_pairs={{0,16},{16,32},{32,48},{48,64},{64,80},{80,96},{96,112},{112,128},... | collective-permute-start | bytes 98312 | tf_op jit(solution)/shard_map/ppermute | solution.py:23
  12.6 499.8 %collective-permute-start = (f32[32,1,256]{2,1,0:T(1,128)S(1)}, f32[32,1,256]{2,1,0:T(1,128)S(1)}, u32[]{:S(2)}, u32[]{:S(2)}) collective-permute-start(f32[32,1,256]{2,1,0:T(1,128)S(1)} %get-tuple-element.18), channel_id=1, source_target_pairs={{16,0},{32,16},{48,32},{64,48},{80,64},{96,80},{112,96},{128,112},... | collective-permute-start | bytes 98312 | tf_op jit(solution)/shard_map/ppermute | solution.py:25
  202.0 5.1 copy-start
  207.1 1.4 copy-start.2
  516.6 7.4 %copy-start.1 = (f32[2,64,256]{2,1,0:T(8,128)S(1)}, f32[2,64,256]{2,1,0:T(8,128)}, u32[]{:S(2)}) copy-start(f32[2,64,256]{2,1,0:T(8,128)} %get-tuple-element.6) | copy-start | bytes 393220
  517.4 6.7 %collective-permute-start.3 = (f32[32,1,256]{2,1,0:T(1,128)S(1)}, f32[32,1,256]{2,1,0:T(1,128)S(1)}, u32[]{:S(2)}, u32[]{:S(2)}) collective-permute-start(f32[32,1,256]{2,1,0:T(1,128)S(1)} %get-tuple-element.11), channel_id=1, source_target_pairs={{0,16},{16,32},{32,48},{48,64},{64,80},{80,96},{96,112},{112,128},... | collective-permute-start | bytes 98312 | tf_op jit(solution)/shard_map/ppermute | solution.py:23
  522.1 9.1 %collective-permute-start.2 = (f32[32,1,256]{2,1,0:T(1,128)S(1)}, f32[32,1,256]{2,1,0:T(1,128)S(1)}, u32[]{:S(2)}, u32[]{:S(2)}) collective-permute-start(f32[32,1,256]{2,1,0:T(1,128)S(1)} %get-tuple-element.12), channel_id=1, source_target_pairs={{16,0},{32,16},{48,32},{64,48},{80,64},{96,80},{112,96},{128,112},... | collective-permute-start | bytes 98312 | tf_op jit(solution)/shard_map/ppermute | solution.py:25
Sparse Core Ops, SparseCore 0:
  202.1 309.2 all-reduce.4
where the time goes:
time: 542 us; the launch traced here: 541 us
  waiting for transfers between devices  310 us (57%)
  blocking collectives  177 us (33%)
  between operations  18.7 us (3%)
  starting transfers between devices  13.5 us (2%)
  local copies, waits for them, and re-layouts  10.8 us (2%)
  other arithmetic  9.42 us (2%)
    psum x1, waiting for transfers between devices, from_root(): return lax.psum(kept, axis)  303 us
    all_gather x2, blocking collectives, body(): lax.all_gather(own_slot, 'space', axis=1, tiled=True).astype(jnp.float32)  177 us
  transfers between devices with their start and end apart: 5, of which 2 were waited for; matrix products, arithmetic and copies ran while one was open for 2% of the time, Pallas kernels for 0%

commit v1 on v0

--- a/solution.py
+++ b/solution.py
@@ -5,6 +5,11 @@
 
 STEPS = 2
 diffusion_scale = 0.24
+
+
+def exchange_gather(x, axis, d):
+    sent = jnp.stack([x] * lax.axis_size(axis))
+    return jnp.concatenate(lax.all_to_all(sent, axis, 0, 0), axis=d)
 
 
 def from_root(value, axis, source):
@@ -72,7 +77,7 @@
         fine_velocity = jnp.einsum(
             "rn,cnz->crz",
             selection,
-            lax.all_gather(own_slot, "space", axis=1, tiled=True).astype(jnp.float32),
+            exchange_gather(own_slot, "space", 1).astype(jnp.float32),
             precision=lax.Precision.HIGHEST,
         )
         result_velocity = from_root(fine_velocity, "scal", owner_index)

time: 542 us -> 352 us (0.65)
  blocking collectives: 177 us -> 29.1 us
  waiting for transfers between devices: 310 us -> 258 us
  starting transfers between devices: 13.5 us -> 22.8 us
    all_gather x2 -> x0, blocking collectives: 177 us -> none  [body(): lax.all_gather(own_slot, 'space', axis=1, tiled=True).astype(jnp.float32)]
    psum x1, waiting for transfers between devices: 303 us -> 251 us  [from_root(): return lax.psum(kept, axis)]
    all_to_all x0 -> x1, blocking collectives: none -> 29.1 us  [exchange_gather(): return jnp.concatenate(lax.all_to_all(sent, axis, 0, 0), axis=d)]
    all_to_all x0 -> x1, starting transfers between devices: none -> 9.67 us  [exchange_gather(): return jnp.concatenate(lax.all_to_all(sent, axis, 0, 0), axis=d)]
  transfers between devices with their start and end apart: 5 -> 6, of which waited for: 2 -> 2; matrix products, arithmetic and copies ran while one was open for 2% -> 3% of each run, Pallas kernels for 0% -> 0%
where the time goes in v1:
time: 352 us
  waiting for transfers between devices  258 us (73%)
  blocking collectives  29.1 us (8%)
  starting transfers between devices  22.8 us (6%)
  between operations  18.7 us (5%)
  local copies, waits for them, and re-layouts  11.5 us (3%)
  other arithmetic  9.42 us (3%)
    psum x1, waiting for transfers between devices, from_root(): return lax.psum(kept, axis)  251 us
    all_to_all x1, blocking collectives, exchange_gather(): return jnp.concatenate(lax.all_to_all(sent, axis, 0, 0), axis=d)  29.1 us
    all_to_all x1, starting transfers between devices, exchange_gather(): return jnp.concatenate(lax.all_to_all(sent, axis, 0, 0), axis=d)  9.67 us
    ppermute x2, starting transfers between devices, padded_2(): lax.ppermute(tail, axis, [(i, (i + 1) % count) for i in range(ends)])  9.27 us
    slice x4, local copies, waits for them, and re-layouts, advance(): east_cell = jnp.roll(center, -1, axis=2)  7.57 us
    ppermute x2, waiting for transfers between devices, padded_2(): lax.ppermute(head, axis, [((i + 1) % count, i) for i in range(ends)])  7.16 us
  transfers between devices with their start and end apart: 6, of which 2 were waited for; matrix products, arithmetic and copies ran while one was open for 3% of the time, Pallas kernels for 0%

profile of v1, /device:TPU:102, one launch (start us, length us, event | category | flops | bytes accessed | tf_op | source)
XLA Modules:
  0.0 351.5 jit_solution(14106403213061034993)
XLA Ops:
  6.5 1.3 fusion.30
  11.7 0.8 dynamic-slice_bitcast_fusion
  12.5 29.1 %all_to_all.10 = bf16[32,2,8,256]{3,2,1,0:T(8,128)(2,1)S(1)} all-to-all(bf16[32,2,8,256]{3,2,1,0:T(8,128)(2,1)S(1)} %stack.5), channel_id=1, replica_groups=mesh['space'=32,'scal'=16] {'space'}, dimensions={0} | all-to-all | bytes 524288 | tf_op jit(solution)/shard_map/all_to_all | solution.py:12
  41.6 0.7 stack.4
  42.3 9.7 %all-to-all-start = ((bf16[32,2,8,256]{3,2,1,0:T(8,128)(2,1)}), bf16[32,2,8,256]{3,2,1,0:T(8,128)(2,1)S(1)}, u32[]{:S(2)}, u32[]{:S(2)}) async-start(bf16[32,2,8,256]{3,2,1,0:T(8,128)(2,1)} %stack.4), calls=%async_computation | async-start | bytes 524288 | tf_op jit(solution)/shard_map/all_to_all | solution.py:12
  52.0 0.0 all-reduce.5.cloned.1.call-start
  52.1 1.1 fusion.27
  53.2 4.6 %collective-permute-start.1 = (f32[32,1,256]{2,1,0:T(1,128)S(1)}, f32[32,1,256]{2,1,0:T(1,128)S(1)}, u32[]{:S(2)}, u32[]{:S(2)}) collective-permute-start(f32[32,1,256]{2,1,0:T(1,128)S(1)} %get-tuple-element.17), channel_id=1, source_target_pairs={{0,16},{16,32},{32,48},{48,64},{64,80},{80,96},{96,112},{112,128},... | collective-permute-start | bytes 98312 | tf_op jit(solution)/shard_map/ppermute | solution.py:28
  57.7 1.9 collective-permute-start
  61.0 0.8 broadcast_add_fusion
  61.8 0.8 broadcast_subtract_fusion
  62.6 0.0 copy-start
  62.6 5.1 %fusion.28 = (f32[32,64,255]{2,1,0:T(8,128)}, f32[32,64,255]{2,1,0:T(8,128)}) fusion(f32[32,64,256]{2,1,0:T(8,128)} %param.6), kind=kLoop, calls=%fused_computation.54 | loop fusion | bytes 8355840 | tf_op jit(solution)/shard_map/jit(_roll_static)/slice | solution.py:41
  67.6 0.9 fusion
  68.6 0.0 all-to-all-done
  68.6 0.9 fusion.1
  69.5 0.0 all-reduce.5.cloned.1.call-update
  69.5 0.0 copy-done
  69.5 0.0 copy-start.2
  69.5 1.4 fusion.29
  70.9 0.0 copy-done.2
  70.9 250.9 %all-reduce.5.cloned.1.call-done = (f32[2,64,256]{2,1,0:T(8,128)}, f32[2,64,256]{2,1,0:T(8,128)}) async-done(((f32[2,64,256]{2,1,0:T(8,128)}, f32[2,64,256]{2,1,0:T(8,128)}), (f32[2,64,256]{2,1,0:T(8,128)}, f32[2,64,256]{2,1,0:T(8,128)})) %all-reduce.5.cloned.1.call-update) | async-done | bytes 262160 | tf_op jit(solution)/shard_map/psum | solution.py:17
  321.8 0.9 fusion.9
  322.7 0.0 collective-permute-done.1
  322.7 0.0 collective-permute-done
  322.7 3.8 %multiply_add_fusion.1 = f32[32,64,256]{2,1,0:T(8,128)S(1)} fusion(f32[32,64,256]{2,1,0:T(8,128)S(1)} %copy-done, f32[32,64,255]{2,1,0:T(8,128)} %get-tuple-element.20, f32[32,64,1]{2,1,0:T(8,128)} %get-tuple-element.22, f32[32,64,1]{2,1,0:T(8,128)S(1)} %get-tuple-element.21, f32[32,64,255]{2,1,0:T(8,128)} %get-tuple-element.19, ...), kind=kLoop, calls=%fused_computation.9 | loop fusion | flops 8912896 | bytes 8585344 | tf_op jit(solution)/shard_map/add | solution.py:45
  326.6 0.4 fusion.26
  327.0 0.0 copy-start.1
  327.0 0.7 fusion.25
  327.7 4.7 %collective-permute-start.3 = (f32[32,1,256]{2,1,0:T(1,128)S(1)}, f32[32,1,256]{2,1,0:T(1,128)S(1)}, u32[]{:S(2)}, u32[]{:S(2)}) collective-permute-start(f32[32,1,256]{2,1,0:T(1,128)S(1)} %get-tuple-element.11), channel_id=1, source_target_pairs={{0,16},{16,32},{32,48},{48,64},{64,80},{80,96},{96,112},{112,128},... | collective-permute-start | bytes 98312 | tf_op jit(solution)/shard_map/ppermute | solution.py:28
  332.4 1.9 collective-permute-start.2
  334.3 0.0 copy-done.1
  334.4 0.0 collective-permute-done.3
  334.4 7.2 %collective-permute-done.2 = f32[32,1,256]{2,1,0:T(1,128)S(1)} collective-permute-done((f32[32,1,256]{2,1,0:T(1,128)S(1)}, f32[32,1,256]{2,1,0:T(1,128)S(1)}, u32[]{:S(2)}, u32[]{:S(2)}) %collective-permute-start.2) | collective-permute-done | bytes 32800 | tf_op jit(solution)/shard_map/ppermute | solution.py:30
  341.5 3.1 multiply_add_fusion
  (4 shorter events, 0.1 us)
Async XLA Ops:
  42.3 26.2 %all-to-all-start = ((bf16[32,2,8,256]{3,2,1,0:T(8,128)(2,1)}), bf16[32,2,8,256]{3,2,1,0:T(8,128)(2,1)S(1)}, u32[]{:S(2)}, u32[]{:S(2)}) async-start(bf16[32,2,8,256]{3,2,1,0:T(8,128)(2,1)} %stack.4), calls=%async_computation | async-start | bytes 524288 | tf_op jit(solution)/shard_map/all_to_all | solution.py:12
  52.0 269.7 %all-reduce.5.cloned.1.call-start = ((), (), s32[]{:S(2)}) async-start(), calls=%async_computation.2 | async-start | bytes 524288 | tf_op jit(solution)/shard_map/psum | solution.py:17
  53.2 269.5 %collective-permute-start.1 = (f32[32,1,256]{2,1,0:T(1,128)S(1)}, f32[32,1,256]{2,1,0:T(1,128)S(1)}, u32[]{:S(2)}, u32[]{:S(2)}) collective-permute-start(f32[32,1,256]{2,1,0:T(1,128)S(1)} %get-tuple-element.17), channel_id=1, source_target_pairs={{0,16},{16,32},{32,48},{48,64},{64,80},{80,96},{96,112},{112,128},... | collective-permute-start | bytes 98312 | tf_op jit(solution)/shard_map/ppermute | solution.py:28
  57.7 264.9 %collective-permute-start = (f32[32,1,256]{2,1,0:T(1,128)S(1)}, f32[32,1,256]{2,1,0:T(1,128)S(1)}, u32[]{:S(2)}, u32[]{:S(2)}) collective-permute-start(f32[32,1,256]{2,1,0:T(1,128)S(1)} %get-tuple-element.18), channel_id=1, source_target_pairs={{16,0},{32,16},{48,32},{64,48},{80,64},{96,80},{112,96},{128,112},... | collective-permute-start | bytes 98312 | tf_op jit(solution)/shard_map/ppermute | solution.py:30
  62.6 7.0 %copy-start = (f32[32,64,256]{2,1,0:T(8,128)S(1)}, f32[32,64,256]{2,1,0:T(8,128)}, u32[]{:S(2)}) copy-start(f32[32,64,256]{2,1,0:T(8,128)} %param.6) | copy-start | bytes 6291460
  69.5 1.4 copy-start.2
  327.0 7.4 %copy-start.1 = (f32[2,64,256]{2,1,0:T(8,128)S(1)}, f32[2,64,256]{2,1,0:T(8,128)}, u32[]{:S(2)}) copy-start(f32[2,64,256]{2,1,0:T(8,128)} %get-tuple-element.6) | copy-start | bytes 393220
  327.7 6.7 %collective-permute-start.3 = (f32[32,1,256]{2,1,0:T(1,128)S(1)}, f32[32,1,256]{2,1,0:T(1,128)S(1)}, u32[]{:S(2)}, u32[]{:S(2)}) collective-permute-start(f32[32,1,256]{2,1,0:T(1,128)S(1)} %get-tuple-element.11), channel_id=1, source_target_pairs={{0,16},{16,32},{32,48},{48,64},{64,80},{80,96},{96,112},{112,128},... | collective-permute-start | bytes 98312 | tf_op jit(solution)/shard_map/ppermute | solution.py:28
  332.4 9.1 %collective-permute-start.2 = (f32[32,1,256]{2,1,0:T(1,128)S(1)}, f32[32,1,256]{2,1,0:T(1,128)S(1)}, u32[]{:S(2)}, u32[]{:S(2)}) collective-permute-start(f32[32,1,256]{2,1,0:T(1,128)S(1)} %get-tuple-element.12), channel_id=1, source_target_pairs={{16,0},{32,16},{48,32},{64,48},{80,64},{96,80},{112,96},{128,112},... | collective-permute-start | bytes 98312 | tf_op jit(solution)/shard_map/ppermute | solution.py:30
Sparse Core Ops, SparseCore 0:
  69.6 252.0 all-reduce.4

commit v2 on v0

--- a/solution.py
+++ b/solution.py
@@ -9,7 +9,7 @@
 
 def from_root(value, axis, source):
     kept = jnp.where(lax.axis_index(axis) == source, value, 0).astype(value.dtype)
-    return lax.psum(kept, axis)
+    return jnp.sum(lax.all_gather(kept, axis), 0)
 
 
 def padded_2(cells, sides, width):

time: 542 us -> 381 us (0.70)
  the two profiles are of different devices: /device:TPU:102 before, /device:TPU:6 now
where the time goes in v2:
time: 381 us
  blocking collectives  236 us (62%)
  waiting for transfers between devices  79.4 us (21%)
  between operations  18.3 us (5%)
  other arithmetic  16.3 us (4%)
  starting transfers between devices  15.5 us (4%)
  local copies, waits for them, and re-layouts  13.3 us (3%)
    all_gather x2, blocking collectives, body(): lax.all_gather(own_slot, 'space', axis=1, tiled=True).astype(jnp.float32)  236 us
    all_gather x2, waiting for transfers between devices, from_root(): return jnp.sum(lax.all_gather(kept, axis), 0)  75.4 us
    ppermute x2, starting transfers between devices, padded_2(): lax.ppermute(head, axis, [((i + 1) % count, i) for i in range(ends)])  11.6 us
    add x2, other arithmetic, advance(): center - velocity[0] * (0.5 * (upper_row - lower_row))  10.6 us
    slice x4, local copies, waits for them, and re-layouts, advance(): east_cell = jnp.roll(center, -1, axis=2)  10.1 us
  transfers between devices with their start and end apart: 6, of which 2 were waited for; matrix products, arithmetic and copies ran while one was open for 5% of the time, Pallas kernels for 0%

profile of v2, /device:TPU:6, one launch (start us, length us, event | category | flops | bytes accessed | tf_op | source)
XLA Modules:
  0.0 380.8 jit_solution(4475491553548812360)
XLA Ops:
  6.5 0.0 all-gather.7.cloned.1.call-start
  6.5 1.3 fusion.28
  12.0 0.8 broadcast_add_fusion
  12.8 0.8 broadcast_subtract_fusion
  13.6 0.8 constant_dynamic-slice_fusion
  14.3 109.1 %all-gather = bf16[1,2,256,256]{3,2,1,0:T(8,128)(2,1)S(1)} all-gather(bf16[1,2,8,256]{3,2,1,0:T(8,128)(2,1)S(1)} %get-tuple-element.26), channel_id=2, replica_groups=mesh['space'=32,'scal'=16] {'space'}, dimensions={2}, use_global_device_ids=true | all-gather | bytes 270336 | tf_op jit(solution)/shard_map/all_gather | solution.py:75
  123.4 0.9 fusion.1
  124.4 0.0 all-gather.7.cloned.1.call-update
  124.4 0.0 all-gather.9.cloned.1.call-start
  125.1 126.9 %all-gather.2 = bf16[1,2,256,256]{3,2,1,0:T(8,128)(2,1)S(1)} all-gather(bf16[1,2,8,256]{3,2,1,0:T(8,128)(2,1)S(1)} %get-tuple-element.25), channel_id=4, replica_groups=mesh['space'=32,'scal'=16] {'space'}, dimensions={2}, use_global_device_ids=true | all-gather | bytes 270336 | tf_op jit(solution)/shard_map/all_gather | solution.py:75
  252.0 0.9 fusion
  253.0 0.0 all-gather.9.cloned.1.call-update
  253.0 1.1 fusion.25
  254.1 1.9 collective-permute-start.1
  256.0 7.7 %collective-permute-start = (f32[32,1,256]{2,1,0:T(1,128)S(1)}, f32[32,1,256]{2,1,0:T(1,128)S(1)}, u32[]{:S(2)}, u32[]{:S(2)}) collective-permute-start(f32[32,1,256]{2,1,0:T(1,128)S(1)} %get-tuple-element.16), channel_id=1, source_target_pairs={{16,0},{32,16},{48,32},{64,48},{80,64},{96,80},{112,96},{128,112},... | collective-permute-start | bytes 98312 | tf_op jit(solution)/shard_map/ppermute | solution.py:25
  263.8 0.7 broadcast_divide_fusion
  264.4 0.0 copy-start
  264.4 3.1 fusion.27
  267.5 0.0 copy-done
  267.5 2.8 fusion.26
  270.3 0.0 all-gather.7.cloned.1.call-done
  270.3 1.7 reduce_sum.18
  272.1 0.0 collective-permute-done.1
  272.1 0.0 collective-permute-done
  272.1 5.9 %multiply_add_fusion.1 = f32[32,64,256]{2,1,0:T(8,128)S(1)} fusion(f32[32,64,256]{2,1,0:T(8,128)} %param.6, f32[32,64,255]{2,1,0:T(8,128)} %get-tuple-element.18, f32[32,64,1]{2,1,0:T(8,128)} %get-tuple-element.20, f32[32,64,1]{2,1,0:T(8,128)S(1)} %get-tuple-element.19, f32[32,64,255]{2,1,0:T(8,128)} %get-tuple-element.17, ...), kind=kLoop, calls=%fused_computation.9 | loop fusion | flops 8912896 | bytes 8585344 | tf_op jit(solution)/shard_map/add | solution.py:40
  278.0 1.4 fusion.24
  279.4 2.8 fusion.23
  282.2 75.4 %all-gather.9.cloned.1.call-done = f32[32,64,256]{2,1,0:T(8,128)} async-done(((f32[2,64,256]{2,1,0:T(8,128)}), f32[32,64,256]{2,1,0:T(8,128)}) %all-gather.9.cloned.1.call-update) | async-done | bytes 2097168 | tf_op jit(solution)/shard_map/all_gather | solution.py:12
  357.7 1.7 reduce_sum.19
  359.4 1.9 collective-permute-start.3
  361.3 3.9 %collective-permute-start.2 = (f32[32,1,256]{2,1,0:T(1,128)S(1)}, f32[32,1,256]{2,1,0:T(1,128)S(1)}, u32[]{:S(2)}, u32[]{:S(2)}) collective-permute-start(f32[32,1,256]{2,1,0:T(1,128)S(1)} %get-tuple-element.10), channel_id=1, source_target_pairs={{16,0},{32,16},{48,32},{64,48},{80,64},{96,80},{112,96},{128,112},... | collective-permute-start | bytes 98312 | tf_op jit(solution)/shard_map/ppermute | solution.py:25
  365.3 0.0 collective-permute-done.3
  365.3 4.0 %collective-permute-done.2 = f32[32,1,256]{2,1,0:T(1,128)S(1)} collective-permute-done((f32[32,1,256]{2,1,0:T(1,128)S(1)}, f32[32,1,256]{2,1,0:T(1,128)S(1)}, u32[]{:S(2)}, u32[]{:S(2)}) %collective-permute-start.2) | collective-permute-done | bytes 32800 | tf_op jit(solution)/shard_map/ppermute | solution.py:25
  369.2 4.8 %multiply_add_fusion = f32[32,64,256]{2,1,0:T(8,128)} fusion(f32[32,64,256]{2,1,0:T(8,128)S(1)} %multiply_add_fusion.1, f32[32,64,255]{2,1,0:T(8,128)} %get-tuple-element.12, f32[32,64,1]{2,1,0:T(8,128)} %get-tuple-element.14, f32[32,64,1]{2,1,0:T(8,128)S(1)} %get-tuple-element.13, f32[32,64,255]{2,1,0:T(8,128)} %get-tuple-element.11, ...), kind=kLoop, calls=%fused_computation.8 | loop fusion | flops 8912896 | bytes 8585344 | tf_op jit(solution)/shard_map/add | solution.py:40
  (3 shorter events, 0.1 us)
Async XLA Ops:
  6.5 263.8 %all-gather.7.cloned.1.call-start = ((), (), s32[]{:S(2)}) async-start(), calls=%async_computation | async-start | bytes 2228224 | tf_op jit(solution)/shard_map/all_gather | solution.py:12
  124.4 233.3 %all-gather.9.cloned.1.call-start = ((), (), s32[]{:S(2)}) async-start(), calls=%async_computation.1 | async-start | bytes 2228224 | tf_op jit(solution)/shard_map/all_gather | solution.py:12
  254.1 18.0 %collective-permute-start.1 = (f32[32,1,256]{2,1,0:T(1,128)S(1)}, f32[32,1,256]{2,1,0:T(1,128)S(1)}, u32[]{:S(2)}, u32[]{:S(2)}) collective-permute-start(f32[32,1,256]{2,1,0:T(1,128)S(1)} %get-tuple-element.15), channel_id=1, source_target_pairs={{0,16},{16,32},{32,48},{48,64},{64,80},{80,96},{96,112},{112,128},... | collective-permute-start | bytes 98312 | tf_op jit(solution)/shard_map/ppermute | solution.py:23
  256.0 16.0 %collective-permute-start = (f32[32,1,256]{2,1,0:T(1,128)S(1)}, f32[32,1,256]{2,1,0:T(1,128)S(1)}, u32[]{:S(2)}, u32[]{:S(2)}) collective-permute-start(f32[32,1,256]{2,1,0:T(1,128)S(1)} %get-tuple-element.16), channel_id=1, source_target_pairs={{16,0},{32,16},{48,32},{64,48},{80,64},{96,80},{112,96},{128,112},... | collective-permute-start | bytes 98312 | tf_op jit(solution)/shard_map/ppermute | solution.py:25
  264.4 3.1 copy-start
  359.4 5.9 %collective-permute-start.3 = (f32[32,1,256]{2,1,0:T(1,128)S(1)}, f32[32,1,256]{2,1,0:T(1,128)S(1)}, u32[]{:S(2)}, u32[]{:S(2)}) collective-permute-start(f32[32,1,256]{2,1,0:T(1,128)S(1)} %get-tuple-element.9), channel_id=1, source_target_pairs={{0,16},{16,32},{32,48},{48,64},{64,80},{80,96},{96,112},{112,128},... | collective-permute-start | bytes 98312 | tf_op jit(solution)/shard_map/ppermute | solution.py:23
  361.3 7.9 %collective-permute-start.2 = (f32[32,1,256]{2,1,0:T(1,128)S(1)}, f32[32,1,256]{2,1,0:T(1,128)S(1)}, u32[]{:S(2)}, u32[]{:S(2)}) collective-permute-start(f32[32,1,256]{2,1,0:T(1,128)S(1)} %get-tuple-element.10), channel_id=1, source_target_pairs={{16,0},{32,16},{48,32},{64,48},{80,64},{96,80},{112,96},{128,112},... | collective-permute-start | bytes 98312 | tf_op jit(solution)/shard_map/ppermute | solution.py:25
Sparse Core Ops, SparseCore 0:
  124.5 104.0 all-gather.6
  253.1 104.4 all-gather.8
